TPU v7x, 256 devices: a whole 4x4x8 slice. The times are simulated.
256 devices in a mesh: dp: 32 (over y, z), tensor: 8 (over x, core).
Axes of the slice: x: 4, y: 4, z: 8, core: 2. Of those that a mesh axis runs over, the one named last changes fastest.
Arguments:
- hidden_in: bfloat16 [1024, 8192], P('dp'), may hold values from -40 to 40
- norm_gain: bfloat16 [8192], P('dp'), may hold values from 0.25 to 2.5
- query_weight: bfloat16 [8192, 8192], P('dp', 'tensor'), may hold values from -0.0625 to 0.0625
- key_weight: bfloat16 [8192, 1024], P('dp', 'tensor'), may hold values from -0.0625 to 0.0625
- value_weight: bfloat16 [8192, 1024], P('dp', 'tensor'), may hold values from -0.0625 to 0.0625
- output_weight: bfloat16 [8192, 8192], P('tensor', 'dp'), may hold values from -0.25 to 0.25
- key_value_cache: bfloat16 [1024, 256, 2, 8, 128], P('dp', None, None, 'tensor'), may hold values from -150 to 150, as said below
- cache_lengths: int32 [1024], replicated, may hold values from 2 to 256, as said below
- parent_beam: int32 [1024], replicated, may hold values from 0 to 1023, as said below
- beam_alive: int32 [1024], replicated, may hold values 0 or 1
Outputs:
- attention_out: bfloat16 [1024, 8192], P(None, 'dp')
Inputs may be any that keep to these rules, and one draw needn't show every extreme that they name: `parent_beam`: among the beams of one device, at most 2 have parents that lie on any one device (beam i lies on device i // 32); on every device some device holds exactly 2 of their parents. `cache_lengths`: some beam holds exactly 256 tokens. `key_value_cache`: slots at or past a beam's length hold arbitrary values.
All inputs are finite; a program needn't handle non-finite values.
Results may differ from a plain program's by a relative error of at most 0.012.
Values may be sent and summed in bfloat16 or wider, within the bound.
No kernel may reach another device: no remote copies, remote signals or barrier semaphores. Data moves between devices by JAX's collectives and lax.ppermute only.
A program may use at most 128 MiB of HBM per device.

v0:
```python
import math
import jax
import jax.numpy as jnp
from jax import lax
from jax.sharding import PartitionSpec as P

HEAD_DIM = 128


def rotate(vectors, position):
    half_width = vectors.shape[-1] // 2
    pair_index = jnp.arange(half_width).astype(jnp.float32)
    frequency = jnp.exp(pair_index * (-2.0 * math.log(1000000.0) / vectors.shape[-1]))
    angles = position.astype(jnp.float32)[:, None] * frequency[None, :]
    cosine = jnp.cos(angles)[:, None, :]
    sine_part = jnp.sin(angles)[:, None, :]
    first_half = vectors[..., :half_width]
    second = vectors[..., half_width:]
    return jnp.concatenate(
        [first_half * cosine - second * sine_part, second * cosine + first_half * sine_part],
        axis=-1,
    )


def attend(queries, key_rows, value_rows, key_new, value_new, length_row):
    row_count, head_total, head_width = queries.shape
    groups = key_rows.shape[2]
    length = key_rows.shape[1]
    grouped = queries.reshape(row_count, groups, head_total // groups, head_width)
    score_scale = 1.0 / math.sqrt(head_width)
    cached = (
        jnp.einsum("rkgd,rlkd->rkgl", grouped, key_rows, preferred_element_type=jnp.float32)
        * score_scale
    )
    latest = (
        jnp.einsum("rkgd,rkd->rkg", grouped, key_new, preferred_element_type=jnp.float32)
        * score_scale
    )
    is_valid = (jnp.arange(length, dtype=jnp.int32)[None, :] < length_row[:, None])[
        :, None, None, :
    ]
    cached = jnp.where(is_valid, cached, -jnp.inf)
    highest = jnp.maximum(jnp.max(cached, axis=-1), latest)
    cached_exp = jnp.exp(cached - highest[..., None])
    latest_exp = jnp.exp(latest - highest)
    denominator = jnp.sum(cached_exp, axis=-1) + latest_exp
    cached_weight = (cached_exp / denominator[..., None]).astype(jnp.bfloat16)
    latest_weight = (latest_exp / denominator).astype(jnp.bfloat16)
    mixture = jnp.einsum(
        "rkgl,rlkd->rkgd", cached_weight, value_rows, preferred_element_type=jnp.float32
    )
    mixture = (
        mixture
        + latest_weight.astype(jnp.float32)[..., None]
        * value_new.astype(jnp.float32)[:, :, None, :]
    )
    return mixture.reshape(row_count, head_total * head_width).astype(jnp.bfloat16)


def arrival_ranks(sources):
    ordinal = jnp.arange(sources.shape[-1], dtype=jnp.int32)
    earlier = (sources[..., None, :] == sources[..., :, None]) & (
        ordinal[None, :] < ordinal[:, None]
    )
    return jnp.sum(earlier.astype(jnp.int32), axis=-1)


def body(
    hidden_in,
    norm_gain,
    query_weight,
    key_weight,
    value_weight,
    output_weight,
    key_value_cache,
    cache_lengths,
    parent_beam,
    beam_alive,
):
    device_count = lax.axis_size("dp")
    device_rank = lax.axis_index("dp")
    local_beams = hidden_in.shape[0]
    capacity = max(2, (2 * local_beams + device_count - 1) // device_count)
    hidden_float = hidden_in.astype(jnp.float32)
    inverse = lax.rsqrt(jnp.mean(hidden_float * hidden_float, axis=1) + 1e-06)
    blocked = lax.all_to_all(hidden_in, "dp", split_axis=1, concat_axis=0, tiled=True)
    scaled = (blocked.astype(jnp.float32) * norm_gain.astype(jnp.float32)[None, :]).astype(
        jnp.bfloat16
    )
    query_width = query_weight.shape[1]
    key_width = key_weight.shape[1]
    summed = (
        lax.psum_scatter(
            jnp.concatenate(
                [
                    jnp.dot(scaled, query_weight, preferred_element_type=jnp.float32),
                    jnp.dot(scaled, key_weight, preferred_element_type=jnp.float32),
                    jnp.dot(scaled, value_weight, preferred_element_type=jnp.float32),
                ],
                axis=1,
            ),
            "dp",
            scatter_dimension=0,
            tiled=True,
        )
        * inverse[:, None]
    )
    first_beam = device_rank * local_beams
    my_parent = lax.dynamic_slice_in_dim(parent_beam, first_beam, local_beams)
    my_alive = lax.dynamic_slice_in_dim(beam_alive, first_beam, local_beams)
    position = jnp.take(cache_lengths, my_parent)
    head_count = query_width // HEAD_DIM
    group_count = key_width // HEAD_DIM
    queries = rotate(
        summed[:, :query_width].reshape(local_beams, head_count, HEAD_DIM), position
    ).astype(jnp.bfloat16)
    key_new = rotate(
        summed[:, query_width : query_width + key_width].reshape(
            local_beams, group_count, HEAD_DIM
        ),
        position,
    ).astype(jnp.bfloat16)
    value_new = (
        summed[:, query_width + key_width :]
        .reshape(local_beams, group_count, HEAD_DIM)
        .astype(jnp.bfloat16)
    )
    source = my_parent // local_beams
    target = source * capacity + arrival_ranks(source)
    slot_total = device_count * capacity
    all_parents = parent_beam.reshape(device_count, local_beams)
    all_sources = all_parents // local_beams
    destination = jnp.broadcast_to(
        jnp.arange(device_count, dtype=jnp.int32)[:, None], (device_count, local_beams)
    )
    placed = jnp.where(
        all_sources == device_rank, destination * capacity + arrival_ranks(all_sources), slot_total
    )
    outgoing = (
        jnp.zeros((slot_total,), jnp.int32)
        .at[placed.reshape(-1)]
        .set((all_parents % local_beams).reshape(-1), mode="drop")
    )
    packed = jnp.take(key_value_cache, outgoing, axis=0)
    arrived = lax.all_to_all(
        packed.reshape((device_count, capacity) + key_value_cache.shape[1:]),
        "dp",
        split_axis=0,
        concat_axis=0,
        tiled=True,
    )
    inherited = jnp.take(arrived.reshape((slot_total,) + key_value_cache.shape[1:]), target, axis=0)
    attention = attend(
        queries, inherited[:, :, 0], inherited[:, :, 1], key_new, value_new, position
    )
    attention = jnp.where(my_alive[:, None] > 0, attention, jnp.zeros_like(attention))
    partial_sum = jnp.dot(
        lax.all_gather(attention, "dp", axis=0, tiled=True),
        output_weight,
        preferred_element_type=jnp.float32,
    )
    return lax.psum(partial_sum, "tensor").astype(jnp.bfloat16)


def solution(mesh):
    placed = (
        P("dp", None),
        P("dp"),
        P("dp", "tensor"),
        P("dp", "tensor"),
        P("dp", "tensor"),
        P("tensor", "dp"),
        P("dp", None, None, "tensor", None),
        P(),
        P(),
        P(),
    )
    return jax.shard_map(body, mesh=mesh, in_specs=placed, out_specs=P(None, "dp"), check_vma=False)
```

profile of v0, /device:TPU:7, one launch (start us, length us, event | category | flops | bytes accessed | tf_op | source)
XLA Modules:
  0.0 547.3 jit_solution(13126944515399061592)
XLA Ops:
  6.5 2.0 copy.55
  8.5 11.2 %all-to-all-start = ((bf16[32,32,256]{2,0,1:T(8,128)(2,1)}), bf16[32,32,256]{2,0,1:T(8,128)(2,1)S(1)}, u32[]{:S(2)}, u32[]{:S(2)}) async-start(bf16[32,32,256]{2,0,1:T(8,128)(2,1)} %bitcast.55), calls=%async_computation | async-start | bytes 1048576 | tf_op jit(solution)/shard_map/all_to_all | solution.py:86
  19.7 0.8 reshape.348
  20.5 0.8 convert_reduce_fusion
  21.5 0.7 add_select_fusion.1
  22.2 4.3 scatter_custom_fusion
  26.5 20.7 %gather_fusion.1 = bf16[64,256,2,128]{3,2,1,0:T(2,128)(2,1)} fusion(bf16[32,256,2,128]{3,2,1,0:T(2,128)(2,1)} %bitcast.57, s32[1024]{0:T(1024)S(1)} %pad_clamp_fusion.1), kind=kCustom, calls=%fused_computation.1 | custom fusion | bytes 16777472 | tf_op jit(solution)/shard_map/jit(_take)/gather | solution.py:144
  47.2 8.9 %copy.41 = bf16[64,256,2,128]{3,1,2,0:T(8,128)(2,1)} copy(bf16[64,256,2,128]{3,2,1,0:T(2,128)(2,1)} %gather_fusion.1) | data formatting | bytes 16777216 | tf_op jit(solution)/shard_map/jit(_take)/gather | solution.py:144
  56.2 7.5 %broadcast_select_fusion = bf16[32,2,256,2,1,128]{5,2,3,1,4,0:T(8,128)(2,1)} fusion(bf16[32,2,256,2,1,128]{5,2,3,1,4,0:T(8,128)(2,1)} %bitcast.56, pred[32,2]{1,0:T(8,128)(4,1)S(1)} %broadcast_in_dim.106), kind=kLoop, calls=%fused_computation.4 | loop fusion | flops 4194304 | bytes 16777280 | tf_op jit(solution)/shard_map/jit(_take)/select_n | solution.py:144
  63.7 9.6 %all-to-all-start.1 = ((bf16[32,2,256,2,1,128]{5,2,3,1,4,0:T(8,128)(2,1)}), bf16[32,2,256,2,1,128]{5,2,3,1,4,0:T(8,128)(2,1)}, u32[]{:S(2)}, u32[]{:S(2)}) async-start(bf16[32,2,256,2,1,128]{5,2,3,1,4,0:T(8,128)(2,1)} %broadcast_select_fusion), calls=%async_computation.1 | async-start | bytes 16777216 | tf_op jit(solution)/shard_map/all_to_all | solution.py:145
  73.5 0.3 fusion.38
  73.8 0.3 fusion.37
  74.1 0.8 fusion.36
  74.9 2.8 pad_maximum_fusion
  77.7 5.9 %copy.45 = f32[1024,1280]{1,0:T(8,128)} copy(f32[1024,1280]{0,1:T(8,128)} %pad_maximum_fusion) | data formatting | bytes 10485760
  83.6 0.2 all-gather.2.cloned.1.call-start
  83.8 0.8 compare_select_fusion.6
  84.6 0.7 gather_fusion
  85.3 0.8 dynamic-slice_compare_fusion
  86.3 0.2 multiply_reduce_fusion
  86.8 306.2 %reduce-scatter.4.cloned.1.call-done = f32[32,1280]{1,0:T(8,128)} async-done(((f32[1024,1280]{1,0:T(8,128)}), f32[32,1280]{1,0:T(8,128)}) %reduce-scatter.4.cloned.1.call-update) | async-done | bytes 163856 | tf_op jit(solution)/shard_map/reduce_scatter | solution.py:93
  392.9 1.0 broadcast_multiply_fusion
  394.3 0.2 fusion.19
  394.6 6.4 %gather_fusion.2 = bf16[32,256,2,128]{3,1,2,0:T(8,128)(2,1)} fusion(bf16[64,256,2,128]{3,1,2,0:T(8,128)(2,1)} %bitcast.4, s32[1024]{0:T(1024)S(1)} %pad_clamp_fusion), kind=kCustom, calls=%fused_computation.2 | custom fusion | bytes 8388736 | tf_op jit(solution)/shard_map/jit(_take)/gather | solution.py:152
  401.0 2.7 bitcast_select_fusion
  403.7 0.8 fusion.35
  404.4 0.2 fusion.7
  404.7 0.5 fusion.5
  405.1 0.7 bitcast_select_fusion.1
  405.9 76.0 %all-gather.2.cloned.1.call-done = bf16[1024,1024]{1,0:T(8,128)(2,1)} async-done(((bf16[32,1024]{1,0:T(8,128)(2,1)}), bf16[1024,1024]{1,0:T(8,128)(2,1)}) %all-gather.2.cloned.1.call-update) | async-done | bytes 2097168 | tf_op jit(solution)/shard_map/all_gather | solution.py:158
  481.9 2.3 fusion.39
  484.2 56.2 %all-reduce.1 = bf16[1024,256]{1,0:T(8,128)(2,1)} all-reduce(f32[1024,256]{1,0:T(8,128)S(1)} %fusion.39), channel_id=1, replica_groups=mesh['dp'=32,'tensor'=8] {'tensor'}, use_global_device_ids=true, to_apply=%region_7.8 | all-reduce | flops 262144 | bytes 1572864 | tf_op jit(solution)/shard_map/psum | solution.py:162
  (50 shorter events, 1.3 us)
Async XLA Ops:
  6.5 67.6 %copy-start = (bf16[256,1024]{1,0:T(8,128)(2,1)S(1)}, bf16[256,1024]{1,0:T(8,128)(2,1)}, u32[]{:S(2)}) copy-start(bf16[256,1024]{1,0:T(8,128)(2,1)} %param.12) | copy-start | bytes 1572868
  8.5 55.2 %all-to-all-start = ((bf16[32,32,256]{2,0,1:T(8,128)(2,1)}), bf16[32,32,256]{2,0,1:T(8,128)(2,1)S(1)}, u32[]{:S(2)}, u32[]{:S(2)}) async-start(bf16[32,32,256]{2,0,1:T(8,128)(2,1)} %bitcast.55), calls=%async_computation | async-start | bytes 1048576 | tf_op jit(solution)/shard_map/all_to_all | solution.py:86
  63.7 9.7 %copy-start.7 = (bf16[256]{0:T(256)(128)(2,1)S(1)}, bf16[256]{0:T(256)(128)(2,1)}, u32[]{:S(2)}) copy-start(bf16[256]{0:T(256)(128)(2,1)} %param.11) | copy-start | bytes 1540
  63.7 9.8 %copy-start.4 = (bf16[256,128]{1,0:T(8,128)(2,1)S(1)}, bf16[256,128]{1,0:T(8,128)(2,1)}, u32[]{:S(2)}) copy-start(bf16[256,128]{1,0:T(8,128)(2,1)} %param.14) | copy-start | bytes 196612
  63.7 10.1 %copy-start.5 = (bf16[256,128]{1,0:T(8,128)(2,1)S(1)}, bf16[256,128]{1,0:T(8,128)(2,1)}, u32[]{:S(2)}) copy-start(bf16[256,128]{1,0:T(8,128)(2,1)} %param.13) | copy-start | bytes 196612
  63.7 330.9 %all-to-all-start.1 = ((bf16[32,2,256,2,1,128]{5,2,3,1,4,0:T(8,128)(2,1)}), bf16[32,2,256,2,1,128]{5,2,3,1,4,0:T(8,128)(2,1)}, u32[]{:S(2)}, u32[]{:S(2)}) async-start(bf16[32,2,256,2,1,128]{5,2,3,1,4,0:T(8,128)(2,1)} %broadcast_select_fusion), calls=%async_computation.1 | async-start | bytes 16777216 | tf_op jit(solution)/shard_map/all_to_all | solution.py:145
  73.3 319.6 %reduce-scatter.4.cloned.1.call-start = ((), (), s32[]{:S(2)}) async-start(), calls=%async_computation.4 | async-start | bytes 5406720 | tf_op jit(solution)/shard_map/reduce_scatter | solution.py:93
  83.6 1.0 copy-start.2
  83.6 2.7 copy-start.3
  83.6 398.3 %all-gather.2.cloned.1.call-start = ((), (), s32[]{:S(2)}) async-start(), calls=%async_computation.3 | async-start | bytes 2162688 | tf_op jit(solution)/shard_map/all_gather | solution.py:158
  403.7 78.2 %copy-start.6 = (bf16[1024,256]{1,0:T(8,128)(2,1)S(1)}, bf16[1024,256]{1,0:T(8,128)(2,1)}, u32[]{:S(2)}) copy-start(bf16[1024,256]{1,0:T(8,128)(2,1)} %param.15) | copy-start | bytes 1572868
  404.7 135.8 %copy-start.1 = (bf16[256,1024]{1,0:T(8,128)(2,1)S(1)}, bf16[256,1024]{1,0:T(8,128)(2,1)}, u32[]{:S(2)}) copy-start(bf16[256,1024]{1,0:T(8,128)(2,1)} %param.12) | copy-start | bytes 1572868
Sparse Core Ops, SparseCore 0:
  83.7 309.1 reduce-scatter.3
  406.0 75.8 all-gather.1
where the time goes:
time: 548 us; the launch traced here: 547 us
  waiting for transfers between devices  382 us (70%)
  blocking collectives  56.2 us (10%)
  local copies, waits for them, and re-layouts  49.8 us (9%)
  starting transfers between devices  21.1 us (4%)
  other arithmetic  19.1 us (3%)
  between operations  13.7 us (2%)
    reduce_scatter x1, waiting for transfers between devices, body(): lax.psum_scatter(jnp.concatenate([jnp.dot(scaled, query_weight, preferred...  306 us
    all_gather x1, waiting for transfers between devices, body(): lax.all_gather(attention, 'dp', axis=0, tiled=True)  76 us
    psum x1, blocking collectives, body(): return lax.psum(partial_sum, 'tensor').astype(jnp.bfloat16)  56.2 us
    gather x2, local copies, waits for them, and re-layouts, body(): packed = jnp.take(key_value_cache, outgoing, axis=0)  29.6 us
    all_to_all x1, starting transfers between devices, body(): lax.all_to_all(hidden_in, 'dp', split_axis=1, concat_axis=0, tiled=True)  11.2 us
  transfers between devices with their start and end apart: 4, of which 2 were waited for; matrix products, arithmetic and copies ran while one was open for 11% of the time, Pallas kernels for 0%

commit v1 on v0

--- a/solution.py
+++ b/solution.py
@@ -3,6 +3,7 @@
 import jax.numpy as jnp
 from jax import lax
 from jax.sharding import PartitionSpec as P
+from jax.lax import all_to_all, axis_size
 
 HEAD_DIM = 128
 
@@ -154,10 +155,19 @@
         queries, inherited[:, :, 0], inherited[:, :, 1], key_new, value_new, position
     )
     attention = jnp.where(my_alive[:, None] > 0, attention, jnp.zeros_like(attention))
+
+    def bind_gates(chunk, peer_axis):
+        num = axis_size(peer_axis)
+        return all_to_all(
+            jnp.tile(chunk, tuple((num if src_i == 0 else 1 for src_i in range(chunk.ndim)))),
+            peer_axis,
+            split_axis=0,
+            concat_axis=0,
+            tiled=True,
+        )
+
     partial_sum = jnp.dot(
-        lax.all_gather(attention, "dp", axis=0, tiled=True),
-        output_weight,
-        preferred_element_type=jnp.float32,
+        bind_gates(attention, "dp"), output_weight, preferred_element_type=jnp.float32
     )
     return lax.psum(partial_sum, "tensor").astype(jnp.bfloat16)
 

time: 548 us -> 528 us (0.964)
  waiting for transfers between devices: 382 us -> 311 us
  blocking collectives: 56.2 us -> 109 us
    all_gather x1 -> x0, waiting for transfers between devices: 76 us -> none  [body(): lax.all_gather(attention, 'dp', axis=0, tiled=True)]
    all_to_all x0 -> x1, blocking collectives: none -> 48.3 us  [bind_gates(): all_to_all(jnp.tile(chunk, tuple((num if src_i == 0 else 1 for src_i in r...]
  transfers between devices with their start and end apart: 4 -> 3, of which waited for: 2 -> 1; matrix products, arithmetic and copies ran while one was open for 11% -> 11% of each run, Pallas kernels for 0% -> 0%
where the time goes in v1:
time: 528 us; the launch traced here: 527 us
  waiting for transfers between devices  311 us (59%)
  blocking collectives  109 us (21%)
  local copies, waits for them, and re-layouts  50.1 us (9%)
  starting transfers between devices  21 us (4%)
  other arithmetic  18.5 us (4%)
  between operations  13.7 us (3%)
    reduce_scatter x1, waiting for transfers between devices, body(): lax.psum_scatter(jnp.concatenate([jnp.dot(scaled, query_weight, preferred...  311 us
    psum x1, blocking collectives, body(): return lax.psum(partial_sum, 'tensor').astype(jnp.bfloat16)  60.8 us
    all_to_all x1, blocking collectives, bind_gates(): all_to_all(jnp.tile(chunk, tuple((num if src_i == 0 else 1 for src_i in r...  48.3 us
    gather x2, local copies, waits for them, and re-layouts, body(): packed = jnp.take(key_value_cache, outgoing, axis=0)  29.6 us
    all_to_all x1, starting transfers between devices, body(): lax.all_to_all(hidden_in, 'dp', split_axis=1, concat_axis=0, tiled=True)  11.2 us
  transfers between devices with their start and end apart: 3, of which 1 were waited for; matrix products, arithmetic and copies ran while one was open for 11% of the time, Pallas kernels for 0%

profile of v1, /device:TPU:7, one launch (start us, length us, event | category | flops | bytes accessed | tf_op | source)
XLA Modules:
  0.0 526.9 jit_solution(16597566094120505863)
XLA Ops:
  6.5 2.0 copy.55
  8.5 11.2 %all-to-all-start = ((bf16[32,32,256]{2,0,1:T(8,128)(2,1)}), bf16[32,32,256]{2,0,1:T(8,128)(2,1)S(1)}, u32[]{:S(2)}, u32[]{:S(2)}) async-start(bf16[32,32,256]{2,0,1:T(8,128)(2,1)} %bitcast.56), calls=%async_computation | async-start | bytes 1048576 | tf_op jit(solution)/shard_map/all_to_all | solution.py:87
  19.7 0.8 reshape.370
  20.5 0.8 convert_reduce_fusion
  21.5 0.7 add_select_fusion.1
  22.2 4.3 scatter_custom_fusion
  26.5 20.7 %gather_fusion.1 = bf16[64,256,2,128]{3,2,1,0:T(2,128)(2,1)} fusion(bf16[32,256,2,128]{3,2,1,0:T(2,128)(2,1)} %bitcast.58, s32[1024]{0:T(1024)S(1)} %pad_clamp_fusion.1), kind=kCustom, calls=%fused_computation.1 | custom fusion | bytes 16777472 | tf_op jit(solution)/shard_map/jit(_take)/gather | solution.py:145
  47.2 8.9 %copy.41 = bf16[64,256,2,128]{3,1,2,0:T(8,128)(2,1)} copy(bf16[64,256,2,128]{3,2,1,0:T(2,128)(2,1)} %gather_fusion.1) | data formatting | bytes 16777216 | tf_op jit(solution)/shard_map/jit(_take)/gather | solution.py:145
  56.2 7.5 %broadcast_select_fusion = bf16[32,2,256,2,1,128]{5,2,3,1,4,0:T(8,128)(2,1)} fusion(bf16[32,2,256,2,1,128]{5,2,3,1,4,0:T(8,128)(2,1)} %bitcast.57, pred[32,2]{1,0:T(8,128)(4,1)S(1)} %broadcast_in_dim.106), kind=kLoop, calls=%fused_computation.4 | loop fusion | flops 4194304 | bytes 16777280 | tf_op jit(solution)/shard_map/jit(_take)/select_n | solution.py:145
  63.7 9.6 %all-to-all-start.1 = ((bf16[32,2,256,2,1,128]{5,2,3,1,4,0:T(8,128)(2,1)}), bf16[32,2,256,2,1,128]{5,2,3,1,4,0:T(8,128)(2,1)}, u32[]{:S(2)}, u32[]{:S(2)}) async-start(bf16[32,2,256,2,1,128]{5,2,3,1,4,0:T(8,128)(2,1)} %broadcast_select_fusion), calls=%async_computation.1 | async-start | bytes 16777216 | tf_op jit(solution)/shard_map/all_to_all | solution.py:146
  73.3 0.2 reduce-scatter.4.cloned.1.call-start
  73.7 0.3 fusion.38
  74.0 0.3 fusion.37
  74.3 0.8 fusion.36
  75.1 2.8 pad_maximum_fusion
  77.9 5.9 %copy.45 = f32[1024,1280]{1,0:T(8,128)} copy(f32[1024,1280]{0,1:T(8,128)} %pad_maximum_fusion) | data formatting | bytes 10485760
  83.8 0.8 compare_select_fusion.6
  84.6 0.7 gather_fusion
  85.3 0.8 dynamic-slice_compare_fusion
  86.3 0.2 multiply_reduce_fusion
  86.8 310.9 %reduce-scatter.4.cloned.1.call-done = f32[32,1280]{1,0:T(8,128)} async-done(((f32[1024,1280]{1,0:T(8,128)}), f32[32,1280]{1,0:T(8,128)}) %reduce-scatter.4.cloned.1.call-update) | async-done | bytes 163856 | tf_op jit(solution)/shard_map/reduce_scatter | solution.py:94
  397.7 1.0 broadcast_multiply_fusion
  399.1 0.2 fusion.19
  399.4 6.4 %gather_fusion.2 = bf16[32,256,2,128]{3,1,2,0:T(8,128)(2,1)} fusion(bf16[64,256,2,128]{3,1,2,0:T(8,128)(2,1)} %bitcast.4, s32[1024]{0:T(1024)S(1)} %pad_clamp_fusion), kind=kCustom, calls=%fused_computation.2 | custom fusion | bytes 8388736 | tf_op jit(solution)/shard_map/jit(_take)/gather | solution.py:153
  405.8 2.7 bitcast_select_fusion
  408.5 0.8 fusion.35
  409.3 0.2 fusion.7
  409.5 0.5 fusion.5
  410.0 0.3 tile.2
  410.3 48.3 %all_to_all.27 = bf16[32,32,1024]{2,1,0:T(8,128)(2,1)S(1)} all-to-all(bf16[32,32,1024]{2,1,0:T(8,128)(2,1)S(1)} %tile.2), channel_id=1, replica_groups=mesh['dp'=32,'tensor'=8] {'dp'}, dimensions={0} | all-to-all | bytes 4194304 | tf_op jit(solution)/shard_map/all_to_all | solution.py:161
  458.6 0.7 fusion.39
  459.3 60.8 %all-reduce.1 = bf16[1024,256]{1,0:T(8,128)(2,1)} all-reduce(f32[1024,256]{1,0:T(8,128)S(1)} %fusion.39), channel_id=1, replica_groups=mesh['dp'=32,'tensor'=8] {'tensor'}, use_global_device_ids=true, to_apply=%region_7.8 | all-reduce | flops 262144 | bytes 1572864 | tf_op jit(solution)/shard_map/psum | solution.py:172
  (49 shorter events, 1.4 us)
Async XLA Ops:
  6.5 67.8 %copy-start = (bf16[256,1024]{1,0:T(8,128)(2,1)S(1)}, bf16[256,1024]{1,0:T(8,128)(2,1)}, u32[]{:S(2)}) copy-start(bf16[256,1024]{1,0:T(8,128)(2,1)} %param.12) | copy-start | bytes 1572868
  8.5 55.2 %all-to-all-start = ((bf16[32,32,256]{2,0,1:T(8,128)(2,1)}), bf16[32,32,256]{2,0,1:T(8,128)(2,1)S(1)}, u32[]{:S(2)}, u32[]{:S(2)}) async-start(bf16[32,32,256]{2,0,1:T(8,128)(2,1)} %bitcast.56), calls=%async_computation | async-start | bytes 1048576 | tf_op jit(solution)/shard_map/all_to_all | solution.py:87
  63.7 9.8 %copy-start.7 = (bf16[256]{0:T(256)(128)(2,1)S(1)}, bf16[256]{0:T(256)(128)(2,1)}, u32[]{:S(2)}) copy-start(bf16[256]{0:T(256)(128)(2,1)} %param.11) | copy-start | bytes 1540
  63.7 10.0 %copy-start.4 = (bf16[256,128]{1,0:T(8,128)(2,1)S(1)}, bf16[256,128]{1,0:T(8,128)(2,1)}, u32[]{:S(2)}) copy-start(bf16[256,128]{1,0:T(8,128)(2,1)} %param.14) | copy-start | bytes 196612
  63.7 10.3 %copy-start.5 = (bf16[256,128]{1,0:T(8,128)(2,1)S(1)}, bf16[256,128]{1,0:T(8,128)(2,1)}, u32[]{:S(2)}) copy-start(bf16[256,128]{1,0:T(8,128)(2,1)} %param.13) | copy-start | bytes 196612
  63.7 335.7 %all-to-all-start.1 = ((bf16[32,2,256,2,1,128]{5,2,3,1,4,0:T(8,128)(2,1)}), bf16[32,2,256,2,1,128]{5,2,3,1,4,0:T(8,128)(2,1)}, u32[]{:S(2)}, u32[]{:S(2)}) async-start(bf16[32,2,256,2,1,128]{5,2,3,1,4,0:T(8,128)(2,1)} %broadcast_select_fusion), calls=%async_computation.1 | async-start | bytes 16777216 | tf_op jit(solution)/shard_map/all_to_all | solution.py:146
  73.3 324.4 %reduce-scatter.4.cloned.1.call-start = ((), (), s32[]{:S(2)}) async-start(), calls=%async_computation.4 | async-start | bytes 5406720 | tf_op jit(solution)/shard_map/reduce_scatter | solution.py:94
  83.8 0.9 copy-start.2
  83.8 2.5 copy-start.3
  409.5 49.1 %copy-start.6 = (bf16[1024,256]{1,0:T(8,128)(2,1)S(1)}, bf16[1024,256]{1,0:T(8,128)(2,1)}, u32[]{:S(2)}) copy-start(bf16[1024,256]{1,0:T(8,128)(2,1)} %param.15) | copy-start | bytes 1572868
  410.3 109.8 %copy-start.1 = (bf16[256,1024]{1,0:T(8,128)(2,1)S(1)}, bf16[256,1024]{1,0:T(8,128)(2,1)}, u32[]{:S(2)}) copy-start(bf16[256,1024]{1,0:T(8,128)(2,1)} %param.12) | copy-start | bytes 1572868
Sparse Core Ops, SparseCore 0:
  83.9 313.7 reduce-scatter.3
